TPU v7x, 128 devices: a whole 4x4x4 slice. The times are simulated.
128 devices in a mesh: req: 4 (over z), seq: 32 (over x, y, core).
Axes of the slice: x: 4, y: 4, z: 4, core: 2. Of those that a mesh axis runs over, the one named last changes fastest.
Arguments:
- short_tokens: bfloat16 [256, 4, 1024], P(('req', 'seq')), may hold values from -6 to 6
- long_tokens: bfloat16 [8, 4, 1024], P('req'), may hold values from -6 to 6
- short_keys: bfloat16 [256, 1024, 1024], P(('req', 'seq'))
- short_values: bfloat16 [256, 1024, 1024], P(('req', 'seq')), may hold values from -6 to 6
- long_keys: bfloat16 [8, 8192, 1024], P('req', 'seq')
- long_values: bfloat16 [8, 8192, 1024], P('req', 'seq'), may hold values from -6 to 6
- short_lengths: int32 [256], P(('req', 'seq')), may hold values from 512 to 1024
- long_lengths: int32 [8], P('req'), may hold values from 4096 to 8192
- attn_gain: float32 [1024], replicated, may hold values from 0.5 to 1.5
- ffn_gain: float32 [1024], replicated, may hold values from 0.5 to 1.5
- w_query: bfloat16 [1024, 1024], P(None, 'req'), may hold values from -0.1875 to 0.1875
- w_key: bfloat16 [1024, 1024], P(None, 'req'), may hold values from -0.1875 to 0.1875
- w_value: bfloat16 [1024, 1024], P(None, 'req'), may hold values from -0.1875 to 0.1875
- w_out: bfloat16 [1024, 1024], P('req'), may hold values from -0.1875 to 0.1875
- w_up: bfloat16 [1024, 4096], P(None, 'req'), may hold values from -0.1875 to 0.1875
- w_down: bfloat16 [4096, 1024], P('req'), may hold values from -0.09375 to 0.09375
Outputs:
- short_hidden: bfloat16 [256, 4, 1024], P(('req', 'seq'))
- long_hidden: bfloat16 [8, 4, 1024], P('req')
- short_new_keys: bfloat16 [256, 4, 1024], P(('req', 'seq'))
- short_new_values: bfloat16 [256, 4, 1024], P(('req', 'seq'))
- long_new_keys: bfloat16 [8, 4, 1024], P('req')
- long_new_values: bfloat16 [8, 4, 1024], P('req')
All inputs are finite; a program needn't handle non-finite values.
Results may differ from a plain program's by a relative error of at most 0.011.
Values may be sent and summed in bfloat16 or wider, within the bound.
No kernel may reach another device: no remote copies, remote signals or barrier semaphores. Data moves between devices by JAX's collectives and lax.ppermute only.
A program may use at most 128 MiB of HBM per device.

v0:
```python
import jax
import jax.numpy as jnp
from jax import lax
from jax.sharding import PartitionSpec as P

H = 16
HD = 64
masked_score = -1e30


def layer_norm(rows, gain):
    mean = jnp.mean(rows, axis=-1, keepdims=True)
    centred = rows - mean
    spread = jnp.mean(centred * centred, axis=-1, keepdims=True)
    return centred * lax.rsqrt(spread + 1e-05) * gain


def partial_block(query, keys, values, valid):
    scores = jnp.einsum("rthd,rphd->rthp", query, keys, preferred_element_type=jnp.float32) * 0.125
    scores = jnp.where(valid, scores, masked_score)
    peak = jnp.max(scores, axis=-1)
    weights = jnp.where(valid, jnp.exp(scores - peak[..., None]), 0.0)
    total = jnp.sum(weights, axis=-1)
    output = jnp.einsum(
        "rthp,rphd->rthd", weights.astype(jnp.bfloat16), values, preferred_element_type=jnp.float32
    )
    return (peak, total, output)


def cache_block(query, keys, values, valid):
    reqs, steps = (query.shape[0], query.shape[1])
    eye = jnp.eye(H, dtype=query.dtype)
    spread = (query[:, :, :, None, :] * eye[None, None, :, :, None]).reshape(
        reqs, steps * H, H * HD
    )
    scores = jnp.einsum("rnc,rpc->rnp", spread, keys, preferred_element_type=jnp.float32) * 0.125
    scores = jnp.where(valid, scores, masked_score)
    peak = jnp.max(scores, axis=-1)
    weights = jnp.where(valid, jnp.exp(scores - peak[..., None]), 0.0)
    total = jnp.sum(weights, axis=-1)
    full = jnp.einsum(
        "rnp,rpc->rnc", weights.astype(jnp.bfloat16), values, preferred_element_type=jnp.float32
    ).reshape(reqs, steps, H, H, HD)
    output = jnp.sum(full * eye.astype(jnp.float32)[None, None, :, :, None], axis=3)
    return (peak.reshape(reqs, steps, H), total.reshape(reqs, steps, H), output)


def join(first, second):
    peak = jnp.maximum(first[0], second[0])
    scale_one = jnp.exp(first[0] - peak)
    scale_two = jnp.exp(second[0] - peak)
    total = first[1] * scale_one + second[1] * scale_two
    output = first[2] * scale_one[..., None] + second[2] * scale_two[..., None]
    return (peak, total, output)


def merge_long(partial_value):
    peak, total, output = partial_value
    packed = jnp.concatenate([output, peak[..., None], total[..., None]], -1)
    size = lax.axis_size("seq")
    me = lax.axis_index("seq")
    width = output.shape[-1]
    distance = 1
    while distance < size:
        pairs = [(i, i ^ distance) for i in range(size)]
        other = lax.ppermute(packed, "seq", pairs)
        lower = me & distance == 0
        first = jnp.where(lower, packed, other)
        second = jnp.where(lower, other, packed)
        top = jnp.maximum(first[..., width], second[..., width])
        scale_one = jnp.exp(first[..., width] - top)[..., None]
        scale_two = jnp.exp(second[..., width] - top)[..., None]
        merged = first[..., :width] * scale_one + second[..., :width] * scale_two
        summed = first[..., width + 1 :] * scale_one + second[..., width + 1 :] * scale_two
        packed = jnp.concatenate([merged, top[..., None], summed], -1)
        distance *= 2
    return (packed[..., width], packed[..., width + 1], packed[..., :width])


def shards(
    short_tokens,
    long_tokens,
    short_keys,
    short_values,
    long_keys,
    long_values,
    short_lengths,
    long_lengths,
    attn_gain,
    ffn_gain,
    w_query,
    w_key,
    w_value,
    w_out,
    w_up,
    w_down,
):
    short_count = short_tokens.shape[0]
    long_count = long_tokens.shape[0]
    steps = short_tokens.shape[1]
    width = short_tokens.shape[2]
    req_count = short_count + long_count
    rows_count = req_count * steps
    groups = lax.axis_size("req")
    block = long_keys.shape[1]
    anchor = lax.axis_index("seq") * block
    short_valid = (jnp.arange(short_keys.shape[1])[None, :] < short_lengths[:, None])[:, None, :]
    long_valid = ((anchor + jnp.arange(block))[None, :] < long_lengths[:, None])[:, None, :]
    w_out_full = lax.all_gather(w_out, "req", axis=0, tiled=True)
    stacked = jnp.concatenate([w_query, w_key, w_value], 1)
    local = w_query.shape[1]
    fresh_ids = jnp.arange(steps)
    fresh_valid = (fresh_ids[None, :] <= fresh_ids[:, None])[None, :, None, :]
    rows = (
        jnp.concatenate([short_tokens, long_tokens], 0)
        .reshape(rows_count, width)
        .astype(jnp.float32)
    )
    normed = layer_norm(rows, attn_gain).astype(jnp.bfloat16)
    project_spread = jnp.dot(
        lax.all_gather(normed, "req", axis=0, tiled=True),
        stacked,
        preferred_element_type=jnp.float32,
    ).astype(jnp.bfloat16)
    moved = lax.all_to_all(project_spread, "req", split_axis=0, concat_axis=1, tiled=True)
    moved = moved.reshape(rows_count, groups, 3, local)
    query = moved[:, :, 0].reshape(req_count, steps, H, HD)
    key_now = moved[:, :, 1].reshape(req_count, steps, width)
    value_now = moved[:, :, 2].reshape(req_count, steps, width)
    fresh_k = key_now.reshape(req_count, steps, H, HD)
    fresh_v = value_now.reshape(req_count, steps, H, HD)
    fresh = partial_block(query, fresh_k, fresh_v, fresh_valid)
    short_part = cache_block(query[:short_count], short_keys, short_values, short_valid)
    long_part = merge_long(cache_block(query[short_count:], long_keys, long_values, long_valid))
    cache_part = jax.tree.map(
        lambda first, second: jnp.concatenate([first, second], 0), short_part, long_part
    )
    peak, total, output = join(cache_part, fresh)
    attended = output / total[..., None]
    attended = attended.reshape(rows_count, width).astype(jnp.bfloat16)
    mixed = rows + jnp.dot(attended, w_out_full, preferred_element_type=jnp.float32)
    normed_ffn = layer_norm(mixed, ffn_gain).astype(jnp.bfloat16)
    hidden = jax.nn.gelu(
        jnp.dot(
            lax.all_gather(normed_ffn, "req", axis=0, tiled=True),
            w_up,
            preferred_element_type=jnp.float32,
        ),
        approximate=False,
    ).astype(jnp.bfloat16)
    result = mixed + lax.psum_scatter(
        jnp.dot(hidden, w_down, preferred_element_type=jnp.float32),
        "req",
        scatter_dimension=0,
        tiled=True,
    )
    states = result.astype(jnp.bfloat16).reshape(req_count, steps, width)
    return (
        states[:short_count],
        states[short_count:],
        key_now[:short_count],
        value_now[:short_count],
        key_now[short_count:],
        value_now[short_count:],
    )


def solution(mesh):
    in_specs = (
        P(("req", "seq"), None, None),
        P("req", None, None),
        P(("req", "seq"), None, None),
        P(("req", "seq"), None, None),
        P("req", "seq", None),
        P("req", "seq", None),
        P(("req", "seq")),
        P("req"),
        P(),
        P(),
        P(None, "req"),
        P(None, "req"),
        P(None, "req"),
        P("req", None),
        P(None, "req"),
        P("req", None),
    )
    out_specs = (
        P(("req", "seq"), None, None),
        P("req", None, None),
        P(("req", "seq"), None, None),
        P(("req", "seq"), None, None),
        P("req", None, None),
        P("req", None, None),
    )
    return jax.shard_map(shards, mesh=mesh, in_specs=in_specs, out_specs=out_specs, check_vma=False)
```

profile of v0, /device:TPU:0, one launch (start us, length us, event | category | flops | bytes accessed | tf_op | source)
XLA Modules:
  0.0 143.6 jit_solution(11437856707310155101)
XLA Ops:
  7.2 0.9 maximum_convert_fusion
  8.1 0.8 fusion.141
  8.9 0.9 multiply_reduce_fusion.3
  10.1 0.8 multiply_convert_fusion.1
  10.8 13.3 %all_gather.9 = bf16[64,1024]{1,0:T(8,128)(2,1)S(1)} all-gather(bf16[16,1024]{1,0:T(8,128)(2,1)S(1)} %multiply_convert_fusion.1), channel_id=1, replica_groups=mesh['req'=4,'seq'=32] {'req'}, dimensions={0}, use_global_device_ids=true | all-gather | bytes 163840 | tf_op jit(solution)/shard_map/all_gather | solution.py:121
  24.1 2.4 %fusion.7 = bf16[64,768]{1,0:T(8,128)(2,1)} fusion(bf16[64,1024]{1,0:T(8,128)(2,1)S(1)} %all_gather.9, bf16[1024,256]{1,0:T(8,128)(2,1)} %param.28, bf16[1024,256]{1,0:T(8,128)(2,1)} %param.27, bf16[1024,256]{1,0:T(8,128)(2,1)} %param.26), kind=kOutput, calls=%fused_computation.8 | convolution fusion | flops 105431040 | bytes 1802240 | tf_op jit(solution)/shard_map/dot_general | solution.py:120
  26.5 4.3 %all-to-all-start = ((bf16[4,16,768]{2,1,0:T(8,128)(2,1)}), bf16[4,16,768]{2,1,0:T(8,128)(2,1)S(1)}, u32[]{:S(2)}, u32[]{:S(2)}) async-start(bf16[4,16,768]{2,1,0:T(8,128)(2,1)} %bitcast), calls=%async_computation | async-start | bytes 196608 | tf_op jit(solution)/shard_map/all_to_all | solution.py:125
  30.8 0.7 all-gather.2.cloned.1.call-update
  31.7 0.2 mul.307
  32.1 0.5 iota_compare_fusion.2
  32.6 4.0 %all-to-all-done = bf16[4,16,768]{2,1,0:T(8,128)(2,1)S(1)} async-done(((bf16[4,16,768]{2,1,0:T(8,128)(2,1)}), bf16[4,16,768]{2,1,0:T(8,128)(2,1)S(1)}, u32[]{:S(2)}, u32[]{:S(2)}) %all-to-all-start) | async-done | bytes 98336 | tf_op jit(solution)/shard_map/all_to_all | solution.py:125
  36.6 0.8 fusion.144
  37.5 0.8 fusion.145
  38.5 0.3 mul.317
  38.8 1.8 %fusion.147 = (f32[2,64]{1,0:T(2,128)S(1)}, f32[2,64,256]{2,1,0:T(8,128)S(1)}) fusion(bf16[2,256,1024]{2,1,0:T(8,128)(2,1)} %param.20, bf16[2,64,1024]{2,1,0:T(8,128)(2,1)S(1)} %mul.317, bf16[64,1024]{1,0:T(8,128)(2,1)S(1)} %mul.307, pred[2,256]{1,0:T(4,128)(4,1)S(1)} %broadcast_compare_fusion), kind=kOutput, calls=%fused_computation.229 | convolution fusion | flops 67338112 | bytes 1573888 | tf_op jit(solution)/shard_map/rnc,rpc->rnp/dot_general | solution.py:36
  40.7 0.2 fusion.72
  40.8 1.6 %fusion.74 = f32[2,64,1024]{2,1,0:T(8,128)S(1)} fusion(bf16[2,256,1024]{2,1,0:T(8,128)(2,1)} %param.21, f32[2,64,256]{2,1,0:T(8,128)S(1)} %get-tuple-element.55, f32[2,64]{1,0:T(2,128)S(1)} %get-tuple-element.54, pred[2,256]{1,0:T(4,128)(4,1)S(1)} %broadcast_compare_fusion), kind=kOutput, calls=%fused_computation.113 | convolution fusion | flops 67207168 | bytes 1704960 | tf_op jit(solution)/shard_map/rnp,rpc->rnc/dot_general | solution.py:41
  42.4 1.3 reshape.257
  43.9 0.3 mul.305
  44.3 4.1 %fusion.148 = (f32[2,64]{1,0:T(2,128)S(1)}, f32[2,64,1024]{2,1,0:T(8,128)S(1)}) fusion(bf16[2,1024,1024]{2,1,0:T(8,128)(2,1)} %param.18, bf16[2,64,1024]{2,1,0:T(8,128)(2,1)S(1)} %mul.305, bf16[64,1024]{1,0:T(8,128)(2,1)S(1)} %mul.307, pred[2,1024]{1,0:T(4,128)(4,1)S(1)} %iota_compare_fusion.1), kind=kOutput, calls=%fused_computation.230 | convolution fusion | flops 268959616 | bytes 5114368 | tf_op jit(solution)/shard_map/rnc,rpc->rnp/dot_general | solution.py:36
  48.3 0.9 fusion.19
  49.3 1.2 reshape.256
  50.5 2.1 %multiply_reduce_fusion.1 = (f32[2,4,16,64]{3,2,1,0:T(8,128)S(1)}, f32[2,4,16,64]{3,2,1,0:T(8,128)S(1)}) fusion(f32[2,4,16,16,64]{4,3,2,1,0:T(8,128)} %reshape.256, f32[16,16]{1,0:T(8,128)S(1)} %fusion.97, f32[2,4,16,16,64]{4,3,2,1,0:T(8,128)} %reshape.257), kind=kLoop, calls=%fused_computation.13 | loop fusion | flops 507904 | bytes 1115136 | tf_op jit(solution)/shard_map/reduce_sum | solution.py:44
  52.7 0.1 copy.305
  53.1 0.1 reshape_reshape_squeeze.6
  53.3 0.7 reshape_squeeze.2
  54.0 1.0 fusion.78
  55.1 0.2 copy.313
  55.2 1.1 broadcast_select_fusion.1
  56.5 1.7 %collective-permute-start.1 = (f32[2,4,16,66]{2,1,3,0:T(4,128)S(1)}, f32[2,4,16,66]{2,1,3,0:T(4,128)S(1)}, u32[]{:S(2)}, u32[]{:S(2)}) collective-permute-start(f32[2,4,16,66]{2,1,3,0:T(4,128)S(1)} %pad_maximum_fusion.1), channel_id=1, source_target_pairs={{0,2},{1,3},{2,0},{3,1},{4,6},{5,7},{6,4},{7,5},{8,10},{9,11},{10,... | collective-permute-start | bytes 101384 | tf_op jit(solution)/shard_map/ppermute | solution.py:66
  58.2 0.1 fusion.84
  58.3 7.2 %collective-permute-done.1 = f32[2,4,16,66]{2,1,3,0:T(4,128)S(1)} collective-permute-done((f32[2,4,16,66]{2,1,3,0:T(4,128)S(1)}, f32[2,4,16,66]{2,1,3,0:T(4,128)S(1)}, u32[]{:S(2)}, u32[]{:S(2)}) %collective-permute-start.1) | collective-permute-done | bytes 33824 | tf_op jit(solution)/shard_map/ppermute | solution.py:66
  65.5 0.1 broadcast_select_fusion.3
  65.8 3.3 %collective-permute-start.2 = (f32[2,4,16,66]{2,1,3,0:T(4,128)S(1)}, f32[2,4,16,66]{2,1,3,0:T(4,128)}, u32[]{:S(2)}, u32[]{:S(2)}) collective-permute-start(f32[2,4,16,66]{2,1,3,0:T(4,128)S(1)} %pad_maximum_fusion.2), channel_id=1, source_target_pairs={{0,4},{1,5},{2,6},{3,7},{4,0},{5,1},{6,2},{7,3},{8,12},{9,13},{10,... | collective-permute-start | bytes 101384 | tf_op jit(solution)/shard_map/ppermute | solution.py:66
  69.1 0.7 fusion.85
  69.8 0.2 copy.319
  70.2 5.5 %collective-permute-done.2 = f32[2,4,16,66]{2,1,3,0:T(4,128)} collective-permute-done((f32[2,4,16,66]{2,1,3,0:T(4,128)S(1)}, f32[2,4,16,66]{2,1,3,0:T(4,128)}, u32[]{:S(2)}, u32[]{:S(2)}) %collective-permute-start.2) | collective-permute-done | bytes 33824 | tf_op jit(solution)/shard_map/ppermute | solution.py:66
  75.6 1.1 broadcast_select_fusion.5
  76.9 1.6 %collective-permute-start.3 = (f32[2,4,16,66]{2,1,3,0:T(4,128)S(1)}, f32[2,4,16,66]{2,1,3,0:T(4,128)S(1)}, u32[]{:S(2)}, u32[]{:S(2)}) collective-permute-start(f32[2,4,16,66]{2,1,3,0:T(4,128)S(1)} %pad_maximum_fusion.3), channel_id=1, source_target_pairs={{0,8},{1,9},{2,10},{3,11},{4,12},{5,13},{6,14},{7,15},{8,0},{9,1},... | collective-permute-start | bytes 101384 | tf_op jit(solution)/shard_map/ppermute | solution.py:66
  78.5 0.2 fusion.76
  78.7 5.6 %collective-permute-done.3 = f32[2,4,16,66]{2,1,3,0:T(4,128)S(1)} collective-permute-done((f32[2,4,16,66]{2,1,3,0:T(4,128)S(1)}, f32[2,4,16,66]{2,1,3,0:T(4,128)S(1)}, u32[]{:S(2)}, u32[]{:S(2)}) %collective-permute-start.3) | collective-permute-done | bytes 33824 | tf_op jit(solution)/shard_map/ppermute | solution.py:66
  84.2 0.1 broadcast_select_fusion.7
  84.5 0.8 pad_maximum_fusion.4
  85.3 3.0 %collective-permute-start.4 = (f32[2,4,16,66]{2,1,3,0:T(4,128)}, f32[2,4,16,66]{2,1,3,0:T(4,128)}, u32[]{:S(2)}, u32[]{:S(2)}) collective-permute-start(f32[2,4,16,66]{2,1,3,0:T(4,128)} %pad_maximum_fusion.4), channel_id=1, source_target_pairs={{0,16},{1,17},{2,18},{3,19},{4,20},{5,21},{6,22},{7,23},{8,24},{9,... | collective-permute-start | bytes 101384 | tf_op jit(solution)/shard_map/ppermute | solution.py:66
  88.3 0.2 fusion.14
  88.7 0.2 copy.308
  88.9 0.2 copy.320
  89.1 4.5 %collective-permute-done.4 = f32[2,4,16,66]{2,1,3,0:T(4,128)} collective-permute-done((f32[2,4,16,66]{2,1,3,0:T(4,128)}, f32[2,4,16,66]{2,1,3,0:T(4,128)}, u32[]{:S(2)}, u32[]{:S(2)}) %collective-permute-start.4) | collective-permute-done | bytes 33824 | tf_op jit(solution)/shard_map/ppermute | solution.py:66
  93.6 1.1 broadcast_select_fusion.9
  94.8 0.2 fusion.13
  95.1 0.1 copy.324
  95.2 0.1 convert_element_type.78
  95.4 2.1 %fusion.149 = (f32[16]{0:T(128)S(1)}, f32[16,1024]{1,0:T(8,128)S(1)}) fusion(f32[16,1024]{1,0:T(8,128)S(1)} %reshape.258, bf16[16,1024]{1,0:T(8,128)(2,1)S(1)} %convert_element_type.78, bf16[1024,1024]{1,0:T(8,128)(2,1)} %all-gather.2.cloned.1.call-done), kind=kOutput, calls=%fused_computation.231 | convolution fusion | flops 33587184 | bytes 2261056 | tf_op jit(solution)/shard_map/dot_general | solution.py:141
  97.5 0.2 multiply_reduce_fusion.2
  97.8 12.0 %all_gather.11 = bf16[64,1024]{1,0:T(8,128)(2,1)S(1)} all-gather(bf16[16,1024]{1,0:T(8,128)(2,1)S(1)} %multiply_convert_fusion), channel_id=1, replica_groups=mesh['req'=4,'seq'=32] {'req'}, dimensions={0}, use_global_device_ids=true | all-gather | bytes 163840 | tf_op jit(solution)/shard_map/all_gather | solution.py:145
  109.8 3.7 %fusion.38 = f32[64,1024]{1,0:T(8,128)} fusion(bf16[1024,1024]{1,0:T(8,128)(2,1)S(1)} %copy-done, bf16[64,1024]{1,0:T(8,128)(2,1)S(1)} %all_gather.11, bf16[1024,1024]{1,0:T(8,128)(2,1)} %param.30), kind=kOutput, calls=%fused_computation.77 | convolution fusion | flops 272695296 | bytes 4587520 | tf_op jit(solution)/shard_map/dot_general | solution.py:152
  113.6 0.6 slice.199
  114.2 0.6 slice.201
  114.8 0.6 slice.203
  115.5 0.6 slice.205
  116.1 18.5 %reduce-scatter.2.cloned.1.call-done = f32[16,1024]{1,0:T(8,128)} async-done(((f32[64,1024]{1,0:T(8,128)}), f32[16,1024]{1,0:T(8,128)}) %reduce-scatter.2.cloned.1.call-update) | async-done | bytes 65552 | tf_op jit(solution)/shard_map/reduce_scatter | solution.py:151
  134.6 0.8 add_convert_fusion
  135.5 0.6 slice.195
  136.1 0.6 slice.197
  (96 shorter events, 2.7 us)
Async XLA Ops:
  7.2 102.6 %copy-start = (bf16[1024,1024]{1,0:T(8,128)(2,1)S(1)}, bf16[1024,1024]{1,0:T(8,128)(2,1)}, u32[]{:S(2)}) copy-start(bf16[1024,1024]{1,0:T(8,128)(2,1)} %param.31) | copy-start | bytes 6291460
  24.1 7.8 %copy-start.16 = (s32[2]{0:T(128)S(1)}, s32[2]{0:T(128)}, u32[]{:S(2)}) copy-start(s32[2]{0:T(128)} %param.22) | copy-start | bytes 28
  24.1 7.9 %copy-start.17 = (s32[2]{0:T(128)S(1)}, s32[2]{0:T(128)}, u32[]{:S(2)}) copy-start(s32[2]{0:T(128)} %param.23) | copy-start | bytes 28
  26.5 10.1 %all-to-all-start = ((bf16[4,16,768]{2,1,0:T(8,128)(2,1)}), bf16[4,16,768]{2,1,0:T(8,128)(2,1)S(1)}, u32[]{:S(2)}, u32[]{:S(2)}) async-start(bf16[4,16,768]{2,1,0:T(8,128)(2,1)} %bitcast), calls=%async_computation | async-start | bytes 196608 | tf_op jit(solution)/shard_map/all_to_all | solution.py:125
  30.8 64.6 %all-gather.2.cloned.1.call-start = ((), (), s32[]{:S(2)}) async-start(), calls=%async_computation.2 | async-start | bytes 2621440 | tf_op jit(solution)/shard_map/all_gather | solution.py:109
  31.5 103.1 %reduce-scatter.2.cloned.1.call-start = ((), (), s32[]{:S(2)}) async-start(), calls=%async_computation.3 | async-start | bytes 327680 | tf_op jit(solution)/shard_map/reduce_scatter | solution.py:151
  44.2 4.1 %copy-start.1 = (bf16[2,1024,1024]{2,1,0:T(8,128)(2,1)S(1)}, bf16[2,1024,1024]{2,1,0:T(8,128)(2,1)}, u32[]{:S(2)}) copy-start(bf16[2,1024,1024]{2,1,0:T(8,128)(2,1)} %param.19) | copy-start | bytes 12582916
  48.3 0.9 copy-start.12
  50.5 2.6 %copy-start.4 = (bf16[16,4,1,256]{3,2,0,1:T(2,128)(2,1)S(1)}, bf16[16,4,1,256]{3,2,0,1:T(2,128)(2,1)}, u32[]{:S(2)}) copy-start(bf16[16,4,1,256]{3,2,0,1:T(2,128)(2,1)} %get-tuple-element.47) | copy-start | bytes 98308
  50.5 2.7 %copy-start.3 = (bf16[16,4,1,256]{3,2,0,1:T(2,128)(2,1)S(1)}, bf16[16,4,1,256]{3,2,0,1:T(2,128)(2,1)}, u32[]{:S(2)}) copy-start(bf16[16,4,1,256]{3,2,0,1:T(2,128)(2,1)} %get-tuple-element.46) | copy-start | bytes 98308
  52.6 5.6 %copy-start.15 = (pred[4,4]{1,0:T(4,128)(4,1)S(1)}, pred[4,4]{1,0:T(4,128)(4,1)}, u32[]{:S(2)}) copy-start(pred[4,4]{1,0:T(4,128)(4,1)} %iota_compare_fusion.2) | copy-start | bytes 52
  53.0 2.2 %collective-permute-start = (f32[2,4,16,66]{2,1,3,0:T(4,128)S(1)}, f32[2,4,16,66]{2,1,3,0:T(4,128)}, u32[]{:S(2)}, u32[]{:S(2)}) collective-permute-start(f32[2,4,16,66]{2,1,3,0:T(4,128)S(1)} %pad_maximum_fusion), channel_id=1, source_target_pairs={{0,1},{1,0},{2,3},{3,2},{4,5},{5,4},{6,7},{7,6},{8,9},{9,8},{10,11... | collective-permute-start | bytes 101384 | tf_op jit(solution)/shard_map/ppermute | solution.py:66
  56.3 13.7 %copy-start.2 = (bf16[16,4,1,256]{3,2,0,1:T(2,128)(2,1)S(1)}, bf16[16,4,1,256]{3,2,0,1:T(2,128)(2,1)}, u32[]{:S(2)}) copy-start(bf16[16,4,1,256]{3,2,0,1:T(2,128)(2,1)} %get-tuple-element.45) | copy-start | bytes 98308
  56.5 8.9 %collective-permute-start.1 = (f32[2,4,16,66]{2,1,3,0:T(4,128)S(1)}, f32[2,4,16,66]{2,1,3,0:T(4,128)S(1)}, u32[]{:S(2)}, u32[]{:S(2)}) collective-permute-start(f32[2,4,16,66]{2,1,3,0:T(4,128)S(1)} %pad_maximum_fusion.1), channel_id=1, source_target_pairs={{0,2},{1,3},{2,0},{3,1},{4,6},{5,7},{6,4},{7,5},{8,10},{9,11},{10,... | collective-permute-start | bytes 101384 | tf_op jit(solution)/shard_map/ppermute | solution.py:66
  58.3 11.5 %copy-start.9 = (f32[4,4,16]{2,1,0:T(4,128)}, f32[4,4,16]{2,1,0:T(4,128)S(1)}, u32[]{:S(2)}) copy-start(f32[4,4,16]{2,1,0:T(4,128)S(1)} %fusion.84) | copy-start | bytes 3076
  65.8 9.8 %collective-permute-start.2 = (f32[2,4,16,66]{2,1,3,0:T(4,128)S(1)}, f32[2,4,16,66]{2,1,3,0:T(4,128)}, u32[]{:S(2)}, u32[]{:S(2)}) collective-permute-start(f32[2,4,16,66]{2,1,3,0:T(4,128)S(1)} %pad_maximum_fusion.2), channel_id=1, source_target_pairs={{0,4},{1,5},{2,6},{3,7},{4,0},{5,1},{6,2},{7,3},{8,12},{9,13},{10,... | collective-permute-start | bytes 101384 | tf_op jit(solution)/shard_map/ppermute | solution.py:66
  76.7 11.6 %copy-start.13 = (f32[2,64]{1,0:T(2,128)S(1)}, f32[2,64]{1,0:T(2,128)}, u32[]{:S(2)}) copy-start(f32[2,64]{1,0:T(2,128)} %copy-done.12) | copy-start | bytes 1540
  76.9 7.3 %collective-permute-start.3 = (f32[2,4,16,66]{2,1,3,0:T(4,128)S(1)}, f32[2,4,16,66]{2,1,3,0:T(4,128)S(1)}, u32[]{:S(2)}, u32[]{:S(2)}) collective-permute-start(f32[2,4,16,66]{2,1,3,0:T(4,128)S(1)} %pad_maximum_fusion.3), channel_id=1, source_target_pairs={{0,8},{1,9},{2,10},{3,11},{4,12},{5,13},{6,14},{7,15},{8,0},{9,1},... | collective-permute-start | bytes 101384 | tf_op jit(solution)/shard_map/ppermute | solution.py:66
  84.4 10.3 %copy-start.10 = (f32[4,4,16]{2,1,0:T(4,128)S(1)}, f32[4,4,16]{2,1,0:T(4,128)}, u32[]{:S(2)}) copy-start(f32[4,4,16]{2,1,0:T(4,128)} %copy-done.9) | copy-start | bytes 3076
  84.4 10.3 %copy-start.11 = (f32[4,4,16]{2,1,0:T(4,128)S(1)}, f32[4,4,16]{2,1,0:T(4,128)}, u32[]{:S(2)}) copy-start(f32[4,4,16]{2,1,0:T(4,128)} %get-tuple-element.48) | copy-start | bytes 3076
  85.3 8.3 %collective-permute-start.4 = (f32[2,4,16,66]{2,1,3,0:T(4,128)}, f32[2,4,16,66]{2,1,3,0:T(4,128)}, u32[]{:S(2)}, u32[]{:S(2)}) collective-permute-start(f32[2,4,16,66]{2,1,3,0:T(4,128)} %pad_maximum_fusion.4), channel_id=1, source_target_pairs={{0,16},{1,17},{2,18},{3,19},{4,20},{5,21},{6,22},{7,23},{8,24},{9,... | collective-permute-start | bytes 101384 | tf_op jit(solution)/shard_map/ppermute | solution.py:66
  94.8 2.9 %copy-start.14 = (f32[1024]{0:T(1024)S(1)}, f32[1024]{0:T(1024)}, u32[]{:S(2)}) copy-start(f32[1024]{0:T(1024)} %param.25) | copy-start | bytes 12292
  109.8 3.8 %copy-start.8 = (bf16[8,4,1,256]{3,2,0,1:T(2,128)(2,1)S(1)}, bf16[8,4,1,256]{3,2,0,1:T(2,128)(2,1)}, u32[]{:S(2)}) copy-start(bf16[8,4,1,256]{3,2,0,1:T(2,128)(2,1)} %get-tuple-element.42) | copy-start | bytes 49156
  109.8 4.4 %copy-start.7 = (bf16[8,4,1,256]{3,2,0,1:T(2,128)(2,1)S(1)}, bf16[8,4,1,256]{3,2,0,1:T(2,128)(2,1)}, u32[]{:S(2)}) copy-start(bf16[8,4,1,256]{3,2,0,1:T(2,128)(2,1)} %get-tuple-element.41) | copy-start | bytes 49156
  109.8 5.0 %copy-start.6 = (bf16[8,4,1,256]{3,2,0,1:T(2,128)(2,1)S(1)}, bf16[8,4,1,256]{3,2,0,1:T(2,128)(2,1)}, u32[]{:S(2)}) copy-start(bf16[8,4,1,256]{3,2,0,1:T(2,128)(2,1)} %get-tuple-element.40) | copy-start | bytes 49156
  109.8 5.7 %copy-start.5 = (bf16[8,4,1,256]{3,2,0,1:T(2,128)(2,1)S(1)}, bf16[8,4,1,256]{3,2,0,1:T(2,128)(2,1)}, u32[]{:S(2)}) copy-start(bf16[8,4,1,256]{3,2,0,1:T(2,128)(2,1)} %get-tuple-element.39) | copy-start | bytes 49156
Sparse Core Ops, SparseCore 0:
  33.3 32.8 all-gather.1
  113.7 20.9 reduce-scatter.1
where the time goes:
time: 144 us
  waiting for transfers between devices  45.9 us (32%)
  blocking collectives  25.3 us (18%)
  matrix products  17.7 us (12%)
  between operations  14.6 us (10%)
  other arithmetic  13.9 us (10%)
  starting transfers between devices  13.9 us (10%)
  local copies, waits for them, and re-layouts  12.2 us (8%)
    ppermute x5, waiting for transfers between devices, merge_long(): other = lax.ppermute(packed, 'seq', pairs)  22.6 us
    reduce_scatter x1, waiting for transfers between devices, shards(): lax.psum_scatter(jnp.dot(hidden, w_down, preferred_element_type=jnp.float...  18.5 us
    all_gather x1, blocking collectives, shards(): lax.all_gather(normed, 'req', axis=0, tiled=True)  13.3 us
    all_gather x1, blocking collectives, shards(): lax.all_gather(normed_ffn, 'req', axis=0, tiled=True)  12 us
    ppermute x5, starting transfers between devices, merge_long(): other = lax.ppermute(packed, 'seq', pairs)  9.6 us
    dot_general x2, matrix products, cache_block(): jnp.einsum('rnc,rpc->rnp', spread, keys, preferred_element_type=jnp.float32)  5.82 us
    all_to_all x1, starting transfers between devices, shards(): lax.all_to_all(project_spread, 'req', split_axis=0, concat_axis=1, tiled=...  4.26 us
    all_to_all x1, waiting for transfers between devices, shards(): lax.all_to_all(project_spread, 'req', split_axis=0, concat_axis=1, tiled=...  4 us
  transfers between devices with their start and end apart: 8, of which 6 were waited for; matrix products, arithmetic and copies ran while one was open for 21% of the time, Pallas kernels for 0%

commit v1 on v0

--- a/solution.py
+++ b/solution.py
@@ -122,7 +122,15 @@
         stacked,
         preferred_element_type=jnp.float32,
     ).astype(jnp.bfloat16)
-    moved = lax.all_to_all(project_spread, "req", split_axis=0, concat_axis=1, tiled=True)
+    moved = jnp.concatenate(
+        jax.lax.all_to_all(
+            jnp.stack(jnp.split(project_spread, jax.lax.axis_size("req"), axis=0), axis=0),
+            "req",
+            0,
+            0,
+        ),
+        axis=1,
+    )
     moved = moved.reshape(rows_count, groups, 3, local)
     query = moved[:, :, 0].reshape(req_count, steps, H, HD)
     key_now = moved[:, :, 1].reshape(req_count, steps, width)

time: 144 us -> 144 us (level)
  no operation moved by 1% of the time
where the time goes in v1:
time: 144 us
  waiting for transfers between devices  45.9 us (32%)
  blocking collectives  25.3 us (18%)
  matrix products  17.1 us (12%)
  other arithmetic  14.6 us (10%)
  between operations  14.6 us (10%)
  starting transfers between devices  13.9 us (10%)
  local copies, waits for them, and re-layouts  12.2 us (8%)
    ppermute x5, waiting for transfers between devices, merge_long(): other = lax.ppermute(packed, 'seq', pairs)  22.6 us
    reduce_scatter x1, waiting for transfers between devices, shards(): lax.psum_scatter(jnp.dot(hidden, w_down, preferred_element_type=jnp.float...  18.5 us
    all_gather x1, blocking collectives, shards(): lax.all_gather(normed, 'req', axis=0, tiled=True)  13.3 us
    all_gather x1, blocking collectives, shards(): lax.all_gather(normed_ffn, 'req', axis=0, tiled=True)  12 us
    ppermute x5, starting transfers between devices, merge_long(): other = lax.ppermute(packed, 'seq', pairs)  9.62 us
    dot_general x2, matrix products, cache_block(): jnp.einsum('rnc,rpc->rnp', spread, keys, preferred_element_type=jnp.float32)  5.82 us
    all_to_all x1, starting transfers between devices, shards(): jax.lax.all_to_all(jnp.stack(jnp.split(project_spread, jax.lax.axis_size(...  4.26 us
    all_to_all x1, waiting for transfers between devices, shards(): jax.lax.all_to_all(jnp.stack(jnp.split(project_spread, jax.lax.axis_size(...  4 us
  transfers between devices with their start and end apart: 8, of which 6 were waited for; matrix products, arithmetic and copies ran while one was open for 21% of the time, Pallas kernels for 0%

profile of v1, /device:TPU:0, one launch (start us, length us, event | category | flops | bytes accessed | tf_op | source)
XLA Modules:
  0.0 143.6 jit_solution(9744866087891835197)
XLA Ops:
  7.2 0.9 maximum_convert_fusion
  8.1 0.8 fusion.141
  8.9 0.9 multiply_reduce_fusion.3
  10.1 0.8 multiply_convert_fusion.1
  10.8 13.3 %all_gather.9 = bf16[64,1024]{1,0:T(8,128)(2,1)S(1)} all-gather(bf16[16,1024]{1,0:T(8,128)(2,1)S(1)} %multiply_convert_fusion.1), channel_id=1, replica_groups=mesh['req'=4,'seq'=32] {'req'}, dimensions={0}, use_global_device_ids=true | all-gather | bytes 163840 | tf_op jit(solution)/shard_map/all_gather | solution.py:121
  24.1 1.8 %fusion.7 = bf16[64,768]{1,0:T(8,128)(2,1)S(1)} fusion(bf16[64,1024]{1,0:T(8,128)(2,1)S(1)} %all_gather.9, bf16[1024,256]{1,0:T(8,128)(2,1)} %param.28, bf16[1024,256]{1,0:T(8,128)(2,1)} %param.27, bf16[1024,256]{1,0:T(8,128)(2,1)} %param.26), kind=kOutput, calls=%fused_computation.8 | convolution fusion | flops 105431040 | bytes 1802240 | tf_op jit(solution)/shard_map/dot_general | solution.py:120
  25.9 0.6 pad_maximum_fusion.5
  26.6 4.3 %all-to-all-start = ((bf16[4,16,768]{2,1,0:T(8,128)(2,1)}), bf16[4,16,768]{2,1,0:T(8,128)(2,1)S(1)}, u32[]{:S(2)}, u32[]{:S(2)}) async-start(bf16[4,16,768]{2,1,0:T(8,128)(2,1)} %pad_maximum_fusion.5), calls=%async_computation | async-start | bytes 196608 | tf_op jit(solution)/shard_map/all_to_all | solution.py:126
  30.8 0.7 all-gather.2.cloned.1.call-update
  31.8 0.2 mul.307
  32.1 0.5 iota_compare_fusion.2
  32.6 4.0 %all-to-all-done = bf16[4,16,768]{2,1,0:T(8,128)(2,1)S(1)} async-done(((bf16[4,16,768]{2,1,0:T(8,128)(2,1)}), bf16[4,16,768]{2,1,0:T(8,128)(2,1)S(1)}, u32[]{:S(2)}, u32[]{:S(2)}) %all-to-all-start) | async-done | bytes 98336 | tf_op jit(solution)/shard_map/all_to_all | solution.py:126
  36.7 0.8 fusion.144
  37.5 0.8 fusion.145
  38.5 0.3 mul.317
  38.8 1.8 %fusion.147 = (f32[2,64]{1,0:T(2,128)S(1)}, f32[2,64,256]{2,1,0:T(8,128)S(1)}) fusion(bf16[2,256,1024]{2,1,0:T(8,128)(2,1)} %param.20, bf16[2,64,1024]{2,1,0:T(8,128)(2,1)S(1)} %mul.317, bf16[64,1024]{1,0:T(8,128)(2,1)S(1)} %mul.307, pred[2,256]{1,0:T(4,128)(4,1)S(1)} %broadcast_compare_fusion), kind=kOutput, calls=%fused_computation.234 | convolution fusion | flops 67338112 | bytes 1573888 | tf_op jit(solution)/shard_map/rnc,rpc->rnp/dot_general | solution.py:36
  40.7 0.2 fusion.72
  40.9 1.6 %fusion.74 = f32[2,64,1024]{2,1,0:T(8,128)S(1)} fusion(bf16[2,256,1024]{2,1,0:T(8,128)(2,1)} %param.21, f32[2,64,256]{2,1,0:T(8,128)S(1)} %get-tuple-element.59, f32[2,64]{1,0:T(2,128)S(1)} %get-tuple-element.58, pred[2,256]{1,0:T(4,128)(4,1)S(1)} %broadcast_compare_fusion), kind=kOutput, calls=%fused_computation.114 | convolution fusion | flops 67207168 | bytes 1704960 | tf_op jit(solution)/shard_map/rnp,rpc->rnc/dot_general | solution.py:41
  42.4 1.3 reshape.253
  43.9 0.3 mul.305
  44.3 4.1 %fusion.148 = (f32[2,64]{1,0:T(2,128)S(1)}, f32[2,64,1024]{2,1,0:T(8,128)S(1)}) fusion(bf16[2,1024,1024]{2,1,0:T(8,128)(2,1)} %param.18, bf16[2,64,1024]{2,1,0:T(8,128)(2,1)S(1)} %mul.305, bf16[64,1024]{1,0:T(8,128)(2,1)S(1)} %mul.307, pred[2,1024]{1,0:T(4,128)(4,1)S(1)} %iota_compare_fusion.1), kind=kOutput, calls=%fused_computation.235 | convolution fusion | flops 268959616 | bytes 5114368 | tf_op jit(solution)/shard_map/rnc,rpc->rnp/dot_general | solution.py:36
  48.4 0.9 fusion.19
  49.3 1.2 reshape.252
  50.5 2.1 %multiply_reduce_fusion.1 = (f32[2,4,16,64]{3,2,1,0:T(8,128)S(1)}, f32[2,4,16,64]{3,2,1,0:T(8,128)S(1)}) fusion(f32[2,4,16,16,64]{4,3,2,1,0:T(8,128)} %reshape.252, f32[16,16]{1,0:T(8,128)S(1)} %fusion.97, f32[2,4,16,16,64]{4,3,2,1,0:T(8,128)} %reshape.253), kind=kLoop, calls=%fused_computation.13 | loop fusion | flops 507904 | bytes 1115136 | tf_op jit(solution)/shard_map/reduce_sum | solution.py:44
  52.7 0.1 copy.305
  53.3 0.7 reshape_squeeze.2
  54.0 1.0 fusion.78
  55.1 0.2 copy.313
  55.3 1.1 broadcast_select_fusion.1
  56.6 1.7 %collective-permute-start.1 = (f32[2,4,16,66]{2,1,3,0:T(4,128)S(1)}, f32[2,4,16,66]{2,1,3,0:T(4,128)S(1)}, u32[]{:S(2)}, u32[]{:S(2)}) collective-permute-start(f32[2,4,16,66]{2,1,3,0:T(4,128)S(1)} %pad_maximum_fusion.1), channel_id=1, source_target_pairs={{0,2},{1,3},{2,0},{3,1},{4,6},{5,7},{6,4},{7,5},{8,10},{9,11},{10,... | collective-permute-start | bytes 101384 | tf_op jit(solution)/shard_map/ppermute | solution.py:66
  58.2 0.1 fusion.84
  58.3 7.2 %collective-permute-done.1 = f32[2,4,16,66]{2,1,3,0:T(4,128)S(1)} collective-permute-done((f32[2,4,16,66]{2,1,3,0:T(4,128)S(1)}, f32[2,4,16,66]{2,1,3,0:T(4,128)S(1)}, u32[]{:S(2)}, u32[]{:S(2)}) %collective-permute-start.1) | collective-permute-done | bytes 33824 | tf_op jit(solution)/shard_map/ppermute | solution.py:66
  65.5 0.1 broadcast_select_fusion.3
  65.8 3.3 %collective-permute-start.2 = (f32[2,4,16,66]{2,1,3,0:T(4,128)S(1)}, f32[2,4,16,66]{2,1,3,0:T(4,128)}, u32[]{:S(2)}, u32[]{:S(2)}) collective-permute-start(f32[2,4,16,66]{2,1,3,0:T(4,128)S(1)} %pad_maximum_fusion.2), channel_id=1, source_target_pairs={{0,4},{1,5},{2,6},{3,7},{4,0},{5,1},{6,2},{7,3},{8,12},{9,13},{10,... | collective-permute-start | bytes 101384 | tf_op jit(solution)/shard_map/ppermute | solution.py:66
  69.1 0.7 fusion.85
  69.8 0.2 copy.319
  70.2 5.4 %collective-permute-done.2 = f32[2,4,16,66]{2,1,3,0:T(4,128)} collective-permute-done((f32[2,4,16,66]{2,1,3,0:T(4,128)S(1)}, f32[2,4,16,66]{2,1,3,0:T(4,128)}, u32[]{:S(2)}, u32[]{:S(2)}) %collective-permute-start.2) | collective-permute-done | bytes 33824 | tf_op jit(solution)/shard_map/ppermute | solution.py:66
  75.6 1.1 broadcast_select_fusion.5
  76.9 1.6 %collective-permute-start.3 = (f32[2,4,16,66]{2,1,3,0:T(4,128)S(1)}, f32[2,4,16,66]{2,1,3,0:T(4,128)S(1)}, u32[]{:S(2)}, u32[]{:S(2)}) collective-permute-start(f32[2,4,16,66]{2,1,3,0:T(4,128)S(1)} %pad_maximum_fusion.3), channel_id=1, source_target_pairs={{0,8},{1,9},{2,10},{3,11},{4,12},{5,13},{6,14},{7,15},{8,0},{9,1},... | collective-permute-start | bytes 101384 | tf_op jit(solution)/shard_map/ppermute | solution.py:66
  78.5 0.2 fusion.76
  78.7 5.6 %collective-permute-done.3 = f32[2,4,16,66]{2,1,3,0:T(4,128)S(1)} collective-permute-done((f32[2,4,16,66]{2,1,3,0:T(4,128)S(1)}, f32[2,4,16,66]{2,1,3,0:T(4,128)S(1)}, u32[]{:S(2)}, u32[]{:S(2)}) %collective-permute-start.3) | collective-permute-done | bytes 33824 | tf_op jit(solution)/shard_map/ppermute | solution.py:66
  84.3 0.1 broadcast_select_fusion.7
  84.5 0.8 pad_maximum_fusion.4
  85.3 3.0 %collective-permute-start.4 = (f32[2,4,16,66]{2,1,3,0:T(4,128)}, f32[2,4,16,66]{2,1,3,0:T(4,128)}, u32[]{:S(2)}, u32[]{:S(2)}) collective-permute-start(f32[2,4,16,66]{2,1,3,0:T(4,128)} %pad_maximum_fusion.4), channel_id=1, source_target_pairs={{0,16},{1,17},{2,18},{3,19},{4,20},{5,21},{6,22},{7,23},{8,24},{9,... | collective-permute-start | bytes 101384 | tf_op jit(solution)/shard_map/ppermute | solution.py:66
  88.3 0.2 fusion.14
  88.7 0.2 copy.308
  88.9 0.2 copy.320
  89.1 4.4 %collective-permute-done.4 = f32[2,4,16,66]{2,1,3,0:T(4,128)} collective-permute-done((f32[2,4,16,66]{2,1,3,0:T(4,128)}, f32[2,4,16,66]{2,1,3,0:T(4,128)}, u32[]{:S(2)}, u32[]{:S(2)}) %collective-permute-start.4) | collective-permute-done | bytes 33824 | tf_op jit(solution)/shard_map/ppermute | solution.py:66
  93.6 1.1 broadcast_select_fusion.9
  94.8 0.2 fusion.13
  95.1 0.1 copy.324
  95.2 0.1 convert_element_type.78
  95.4 2.1 %fusion.149 = (f32[16]{0:T(128)S(1)}, f32[16,1024]{1,0:T(8,128)S(1)}) fusion(f32[16,1024]{1,0:T(8,128)S(1)} %reshape.254, bf16[16,1024]{1,0:T(8,128)(2,1)S(1)} %convert_element_type.78, bf16[1024,1024]{1,0:T(8,128)(2,1)} %all-gather.2.cloned.1.call-done), kind=kOutput, calls=%fused_computation.236 | convolution fusion | flops 33587184 | bytes 2261056 | tf_op jit(solution)/shard_map/dot_general | solution.py:149
  97.5 0.2 multiply_reduce_fusion.2
  97.8 12.0 %all_gather.11 = bf16[64,1024]{1,0:T(8,128)(2,1)S(1)} all-gather(bf16[16,1024]{1,0:T(8,128)(2,1)S(1)} %multiply_convert_fusion), channel_id=1, replica_groups=mesh['req'=4,'seq'=32] {'req'}, dimensions={0}, use_global_device_ids=true | all-gather | bytes 163840 | tf_op jit(solution)/shard_map/all_gather | solution.py:153
  109.8 3.7 %fusion.38 = f32[64,1024]{1,0:T(8,128)} fusion(bf16[1024,1024]{1,0:T(8,128)(2,1)S(1)} %copy-done, bf16[64,1024]{1,0:T(8,128)(2,1)S(1)} %all_gather.11, bf16[1024,1024]{1,0:T(8,128)(2,1)} %param.30), kind=kOutput, calls=%fused_computation.77 | convolution fusion | flops 272695296 | bytes 4587520 | tf_op jit(solution)/shard_map/dot_general | solution.py:160
  113.6 0.6 slice.199
  114.2 0.6 slice.201
  114.9 0.6 slice.203
  115.5 0.6 slice.205
  116.1 18.5 %reduce-scatter.2.cloned.1.call-done = f32[16,1024]{1,0:T(8,128)} async-done(((f32[64,1024]{1,0:T(8,128)}), f32[16,1024]{1,0:T(8,128)}) %reduce-scatter.2.cloned.1.call-update) | async-done | bytes 65552 | tf_op jit(solution)/shard_map/reduce_scatter | solution.py:159
  134.6 0.8 add_convert_fusion
  135.5 0.6 slice.195
  136.1 0.6 slice.197
  (98 shorter events, 2.8 us)
Async XLA Ops:
  7.2 102.6 %copy-start = (bf16[1024,1024]{1,0:T(8,128)(2,1)S(1)}, bf16[1024,1024]{1,0:T(8,128)(2,1)}, u32[]{:S(2)}) copy-start(bf16[1024,1024]{1,0:T(8,128)(2,1)} %param.31) | copy-start | bytes 6291460
  24.1 7.8 %copy-start.16 = (s32[2]{0:T(128)S(1)}, s32[2]{0:T(128)}, u32[]{:S(2)}) copy-start(s32[2]{0:T(128)} %param.22) | copy-start | bytes 28
  24.1 7.9 %copy-start.17 = (s32[2]{0:T(128)S(1)}, s32[2]{0:T(128)}, u32[]{:S(2)}) copy-start(s32[2]{0:T(128)} %param.23) | copy-start | bytes 28
  26.6 10.1 %all-to-all-start = ((bf16[4,16,768]{2,1,0:T(8,128)(2,1)}), bf16[4,16,768]{2,1,0:T(8,128)(2,1)S(1)}, u32[]{:S(2)}, u32[]{:S(2)}) async-start(bf16[4,16,768]{2,1,0:T(8,128)(2,1)} %pad_maximum_fusion.5), calls=%async_computation | async-start | bytes 196608 | tf_op jit(solution)/shard_map/all_to_all | solution.py:126
  30.8 64.6 %all-gather.2.cloned.1.call-start = ((), (), s32[]{:S(2)}) async-start(), calls=%async_computation.2 | async-start | bytes 2621440 | tf_op jit(solution)/shard_map/all_gather | solution.py:109
  31.6 103.1 %reduce-scatter.2.cloned.1.call-start = ((), (), s32[]{:S(2)}) async-start(), calls=%async_computation.3 | async-start | bytes 327680 | tf_op jit(solution)/shard_map/reduce_scatter | solution.py:159
  44.3 4.1 %copy-start.1 = (bf16[2,1024,1024]{2,1,0:T(8,128)(2,1)S(1)}, bf16[2,1024,1024]{2,1,0:T(8,128)(2,1)}, u32[]{:S(2)}) copy-start(bf16[2,1024,1024]{2,1,0:T(8,128)(2,1)} %param.19) | copy-start | bytes 12582916
  48.3 0.9 copy-start.12
  50.5 2.6 %copy-start.4 = (bf16[16,4,1,256]{3,2,0,1:T(2,128)(2,1)S(1)}, bf16[16,4,1,256]{3,2,0,1:T(2,128)(2,1)}, u32[]{:S(2)}) copy-start(bf16[16,4,1,256]{3,2,0,1:T(2,128)(2,1)} %get-tuple-element.47) | copy-start | bytes 98308
  50.5 2.7 %copy-start.3 = (bf16[16,4,1,256]{3,2,0,1:T(2,128)(2,1)S(1)}, bf16[16,4,1,256]{3,2,0,1:T(2,128)(2,1)}, u32[]{:S(2)}) copy-start(bf16[16,4,1,256]{3,2,0,1:T(2,128)(2,1)} %get-tuple-element.46) | copy-start | bytes 98308
  52.7 5.6 %copy-start.15 = (pred[4,4]{1,0:T(4,128)(4,1)S(1)}, pred[4,4]{1,0:T(4,128)(4,1)}, u32[]{:S(2)}) copy-start(pred[4,4]{1,0:T(4,128)(4,1)} %iota_compare_fusion.2) | copy-start | bytes 52
  53.0 2.3 %collective-permute-start = (f32[2,4,16,66]{2,1,3,0:T(4,128)S(1)}, f32[2,4,16,66]{2,1,3,0:T(4,128)}, u32[]{:S(2)}, u32[]{:S(2)}) collective-permute-start(f32[2,4,16,66]{2,1,3,0:T(4,128)S(1)} %pad_maximum_fusion), channel_id=1, source_target_pairs={{0,1},{1,0},{2,3},{3,2},{4,5},{5,4},{6,7},{7,6},{8,9},{9,8},{10,11... | collective-permute-start | bytes 101384 | tf_op jit(solution)/shard_map/ppermute | solution.py:66
  56.4 13.7 %copy-start.2 = (bf16[16,4,1,256]{3,2,0,1:T(2,128)(2,1)S(1)}, bf16[16,4,1,256]{3,2,0,1:T(2,128)(2,1)}, u32[]{:S(2)}) copy-start(bf16[16,4,1,256]{3,2,0,1:T(2,128)(2,1)} %get-tuple-element.45) | copy-start | bytes 98308
  56.6 8.9 %collective-permute-start.1 = (f32[2,4,16,66]{2,1,3,0:T(4,128)S(1)}, f32[2,4,16,66]{2,1,3,0:T(4,128)S(1)}, u32[]{:S(2)}, u32[]{:S(2)}) collective-permute-start(f32[2,4,16,66]{2,1,3,0:T(4,128)S(1)} %pad_maximum_fusion.1), channel_id=1, source_target_pairs={{0,2},{1,3},{2,0},{3,1},{4,6},{5,7},{6,4},{7,5},{8,10},{9,11},{10,... | collective-permute-start | bytes 101384 | tf_op jit(solution)/shard_map/ppermute | solution.py:66
  58.3 11.5 %copy-start.9 = (f32[4,4,16]{2,1,0:T(4,128)}, f32[4,4,16]{2,1,0:T(4,128)S(1)}, u32[]{:S(2)}) copy-start(f32[4,4,16]{2,1,0:T(4,128)S(1)} %fusion.84) | copy-start | bytes 3076
  65.8 9.8 %collective-permute-start.2 = (f32[2,4,16,66]{2,1,3,0:T(4,128)S(1)}, f32[2,4,16,66]{2,1,3,0:T(4,128)}, u32[]{:S(2)}, u32[]{:S(2)}) collective-permute-start(f32[2,4,16,66]{2,1,3,0:T(4,128)S(1)} %pad_maximum_fusion.2), channel_id=1, source_target_pairs={{0,4},{1,5},{2,6},{3,7},{4,0},{5,1},{6,2},{7,3},{8,12},{9,13},{10,... | collective-permute-start | bytes 101384 | tf_op jit(solution)/shard_map/ppermute | solution.py:66
  76.7 11.6 %copy-start.13 = (f32[2,64]{1,0:T(2,128)S(1)}, f32[2,64]{1,0:T(2,128)}, u32[]{:S(2)}) copy-start(f32[2,64]{1,0:T(2,128)} %copy-done.12) | copy-start | bytes 1540
  76.9 7.3 %collective-permute-start.3 = (f32[2,4,16,66]{2,1,3,0:T(4,128)S(1)}, f32[2,4,16,66]{2,1,3,0:T(4,128)S(1)}, u32[]{:S(2)}, u32[]{:S(2)}) collective-permute-start(f32[2,4,16,66]{2,1,3,0:T(4,128)S(1)} %pad_maximum_fusion.3), channel_id=1, source_target_pairs={{0,8},{1,9},{2,10},{3,11},{4,12},{5,13},{6,14},{7,15},{8,0},{9,1},... | collective-permute-start | bytes 101384 | tf_op jit(solution)/shard_map/ppermute | solution.py:66
  84.4 10.3 %copy-start.10 = (f32[4,4,16]{2,1,0:T(4,128)S(1)}, f32[4,4,16]{2,1,0:T(4,128)}, u32[]{:S(2)}) copy-start(f32[4,4,16]{2,1,0:T(4,128)} %copy-done.9) | copy-start | bytes 3076
  84.4 10.3 %copy-start.11 = (f32[4,4,16]{2,1,0:T(4,128)S(1)}, f32[4,4,16]{2,1,0:T(4,128)}, u32[]{:S(2)}) copy-start(f32[4,4,16]{2,1,0:T(4,128)} %get-tuple-element.52) | copy-start | bytes 3076
  85.3 8.3 %collective-permute-start.4 = (f32[2,4,16,66]{2,1,3,0:T(4,128)}, f32[2,4,16,66]{2,1,3,0:T(4,128)}, u32[]{:S(2)}, u32[]{:S(2)}) collective-permute-start(f32[2,4,16,66]{2,1,3,0:T(4,128)} %pad_maximum_fusion.4), channel_id=1, source_target_pairs={{0,16},{1,17},{2,18},{3,19},{4,20},{5,21},{6,22},{7,23},{8,24},{9,... | collective-permute-start | bytes 101384 | tf_op jit(solution)/shard_map/ppermute | solution.py:66
  94.8 2.9 %copy-start.14 = (f32[1024]{0:T(1024)S(1)}, f32[1024]{0:T(1024)}, u32[]{:S(2)}) copy-start(f32[1024]{0:T(1024)} %param.25) | copy-start | bytes 12292
  109.8 3.8 %copy-start.8 = (bf16[8,4,1,256]{3,2,0,1:T(2,128)(2,1)S(1)}, bf16[8,4,1,256]{3,2,0,1:T(2,128)(2,1)}, u32[]{:S(2)}) copy-start(bf16[8,4,1,256]{3,2,0,1:T(2,128)(2,1)} %get-tuple-element.42) | copy-start | bytes 49156
  109.8 4.4 %copy-start.7 = (bf16[8,4,1,256]{3,2,0,1:T(2,128)(2,1)S(1)}, bf16[8,4,1,256]{3,2,0,1:T(2,128)(2,1)}, u32[]{:S(2)}) copy-start(bf16[8,4,1,256]{3,2,0,1:T(2,128)(2,1)} %get-tuple-element.41) | copy-start | bytes 49156
  109.8 5.0 %copy-start.6 = (bf16[8,4,1,256]{3,2,0,1:T(2,128)(2,1)S(1)}, bf16[8,4,1,256]{3,2,0,1:T(2,128)(2,1)}, u32[]{:S(2)}) copy-start(bf16[8,4,1,256]{3,2,0,1:T(2,128)(2,1)} %get-tuple-element.40) | copy-start | bytes 49156
  109.8 5.7 %copy-start.5 = (bf16[8,4,1,256]{3,2,0,1:T(2,128)(2,1)S(1)}, bf16[8,4,1,256]{3,2,0,1:T(2,128)(2,1)}, u32[]{:S(2)}) copy-start(bf16[8,4,1,256]{3,2,0,1:T(2,128)(2,1)} %get-tuple-element.39) | copy-start | bytes 49156
Sparse Core Ops, SparseCore 0:
  33.3 32.8 all-gather.1
  113.7 20.9 reduce-scatter.1
